TPU v7x, 512 devices: a whole 4x8x8 slice. The times are simulated.
512 devices in a mesh: section: 8 (over y), dp: 64 (over x, z, core).
Axes of the slice: x: 4, y: 8, z: 8, core: 2. Of those that a mesh axis runs over, the one named last changes fastest.
Arguments:
- queries: bfloat16 [65536, 3584], P(('section', 'dp')), may hold values from -1 to 1
- passages: bfloat16 [128, 64, 3584], P('dp'), may hold values from -1 to 1
- candidates: int32 [512, 3], P('section'), may hold values from 0 to 63, as said below
- counts: int32 [512], P('section'), may hold values from 1 to 3, 1024 in all
- teacher: float32 [65536, 384], P(('section', 'dp')), may hold values from -20 to 450
- section_weights: bfloat16 [8, 3584, 3584], P('section', 'dp'), may hold values from -0.09375 to 0.09375
- section_inputs: bfloat16 [8, 64, 3584], P('section', None, 'dp'), may hold values from -1.5 to 1.5
- pre_acts: bfloat16 [8, 64, 3584], P('section', None, 'dp'), may hold values from -8 to 8
Outputs:
- query_grads: bfloat16 [65536, 3584], P(('section', 'dp'))
- passage_grads: bfloat16 [128, 64, 3584], P('dp')
- grad_inputs: float32 [8, 64, 3584], P('section', None, 'dp')
- weight_grads: bfloat16 [8, 3584, 3584], P('section', 'dp')
Inputs may be any that keep to these rules, and one draw needn't show every extreme that they name: `candidates`: each row names 3 different passage blocks. A query block uses the first counts[b] entries of its row of candidates.
All inputs are finite; a program needn't handle non-finite values.
Results may differ from a plain program's by a relative error of at most 0.0085.
Values may be sent and summed in bfloat16 or wider, within the bound.
No kernel may reach another device: no remote copies, remote signals or barrier semaphores. Data moves between devices by JAX's collectives and lax.ppermute only.
A program may use at most 64 MiB of HBM per device.

v0:
```python
import jax
import jax.numpy as jnp
from jax import lax
from jax.sharding import PartitionSpec as P

INVERSE_TEMP = 20.0


def passed_along(value, axis, steps):
    count = lax.axis_size(axis)
    initial, last = (max(0, -steps), min(count, count - steps))
    return lax.ppermute(value, axis, [(source, source + steps) for source in range(initial, last)])


def soft_weights(logits, valid):
    masked = jnp.where(valid, logits, -1e30)
    highest = jnp.max(masked, axis=-1, keepdims=True)
    expons = jnp.where(valid, jnp.exp(masked - highest), 0.0)
    return expons / jnp.sum(expons, axis=-1, keepdims=True)


def body(queries, passages, candidates, counts, teacher, section_weights, section_inputs, pre_acts):
    dp_count = lax.axis_size("dp")
    dp_index = lax.axis_index("dp")
    stripe, block_total, width = passages.shape
    row_block_count = stripe * dp_count
    blocks_here = candidates.shape[0] // dp_count
    slot_count = candidates.shape[1]
    requests = blocks_here * slot_count
    all_slots = candidates.reshape(-1)
    outgoing = jnp.take(passages, all_slots, axis=1)
    pulled_rows = lax.all_to_all(outgoing, "dp", split_axis=1, concat_axis=0, tiled=True)
    pulled_rows = pulled_rows.reshape(row_block_count, blocks_here, slot_count, width)
    own_counts = lax.dynamic_slice_in_dim(counts, dp_index * blocks_here, blocks_here)
    slot_valid = jnp.arange(slot_count, dtype=jnp.int32)[None, :] < own_counts[:, None]
    column_valid = jnp.repeat(slot_valid, row_block_count, axis=1)[:, None, :]
    query_row_items = queries.reshape(blocks_here, row_block_count, width)
    logits = (
        jnp.einsum(
            "ixp,wifp->ixfw", query_row_items, pulled_rows, preferred_element_type=jnp.float32
        )
        * INVERSE_TEMP
    )
    logits = logits.reshape(blocks_here, row_block_count, slot_count * row_block_count)
    target_logits = soft_weights(
        teacher.reshape(blocks_here, row_block_count, slot_count * row_block_count), column_valid
    )
    weight_matrices = (soft_weights(logits, column_valid) - target_logits).astype(jnp.bfloat16)
    weight_matrices = weight_matrices.reshape(
        blocks_here, row_block_count, slot_count, row_block_count
    )
    query_sums = (
        jnp.einsum(
            "geal,lgay->gey", weight_matrices, pulled_rows, preferred_element_type=jnp.float32
        )
        * INVERSE_TEMP
    )
    passage_sums = (
        jnp.einsum(
            "fnyw,fnj->wfyj", weight_matrices, query_row_items, preferred_element_type=jnp.float32
        )
        * INVERSE_TEMP
    )
    block_terms = passage_sums.reshape(row_block_count, requests, width).astype(jnp.bfloat16)
    micro_count = section_inputs.shape[1] // dp_count
    col_width = width // dp_count
    micro_cols = jnp.transpose(
        query_sums[0, :micro_count].reshape(micro_count, dp_count, col_width), (1, 0, 2)
    )
    incoming_piece = lax.all_to_all(block_terms, "dp", split_axis=0, concat_axis=1, tiled=True)
    entry = lax.all_to_all(micro_cols, "dp", split_axis=0, concat_axis=1, tiled=True)
    onehot = (all_slots[:, None] == jnp.arange(block_total, dtype=jnp.int32)[None, :]).astype(
        jnp.float32
    )
    dense = jnp.einsum(
        "sjd,jn->snd",
        incoming_piece.astype(jnp.float32),
        onehot,
        precision=lax.Precision.HIGHEST,
        preferred_element_type=jnp.float32,
    )
    passage_out = lax.psum(dense, "section").astype(jnp.bfloat16)
    weight_rows = section_weights[0]
    input_cols = section_inputs[0]
    pre = pre_acts[0].astype(jnp.float32)
    sigma = jax.nn.sigmoid(pre)
    slope = sigma * (1.0 + pre * (1.0 - sigma))
    carry = entry.reshape(dp_count * micro_count, col_width)
    section_count = lax.axis_size("section")
    section_index = lax.axis_index("section")
    grad_cols = jnp.zeros_like(carry)
    grad_weight = jnp.zeros((col_width, width), jnp.float32)
    for section_turn in range(section_count):
        active_flag = section_count - 1 - section_turn
        inner = (carry * slope).astype(jnp.bfloat16)
        piece = lax.all_gather(inner, "dp", axis=1, tiled=True)
        back_sum = jnp.einsum("mj,ij->mi", piece, weight_rows, preferred_element_type=jnp.float32)
        weight_part = jnp.einsum("mi,mj->ij", input_cols, piece, preferred_element_type=jnp.float32)
        back_sum, layer_weight = (back_sum, weight_part)
        updated = carry + back_sum
        is_active = section_index == active_flag
        grad_cols = jnp.where(is_active, updated, grad_cols)
        grad_weight = jnp.where(is_active, layer_weight, grad_weight)
        if section_turn + 1 < section_count:
            carry = passed_along(updated, "section", -1)
    return (
        query_sums.reshape(blocks_here * row_block_count, width).astype(jnp.bfloat16),
        passage_out,
        grad_cols[None],
        grad_weight[None].astype(jnp.bfloat16),
    )


def solution(mesh):
    placed = (
        P(("section", "dp"), None),
        P("dp", None, None),
        P("section", None),
        P("section"),
        P(("section", "dp"), None),
        P("section", "dp", None),
        P("section", None, "dp"),
        P("section", None, "dp"),
    )
    return jax.shard_map(
        body,
        mesh=mesh,
        in_specs=placed,
        out_specs=(
            P(("section", "dp"), None),
            P("dp", None, None),
            P("section", None, "dp"),
            P("section", "dp", None),
        ),
        check_vma=False,
    )
```

profile of v0, /device:TPU:16, one launch (start us, length us, event | category | flops | bytes accessed | tf_op | source)
XLA Modules:
  0.0 732.7 jit_solution(10540011991136659404)
XLA Ops:
  1.8 15.2 %gather_fusion = bf16[192,2,3584]{2,0,1:T(8,128)(2,1)} fusion(bf16[2,64,3584]{2,1,0:T(8,128)(2,1)} %param.9, s32[1024]{0:T(1024)S(1)} %pad_clamp_fusion), kind=kCustom, calls=%fused_computation | custom fusion | bytes 5505792 | tf_op jit(solution)/shard_map/jit(_take)/gather | solution.py:31
  17.0 2.1 select_bitcast_fusion
  19.1 4.4 copy.29
  23.5 14.1 %all-to-all-start = ((bf16[2,192,3584]{2,0,1:T(2,128)(2,1)}), bf16[2,192,3584]{2,0,1:T(2,128)(2,1)}, u32[]{:S(2)}, u32[]{:S(2)}) async-start(bf16[2,192,3584]{2,0,1:T(2,128)(2,1)} %copy.29), calls=%async_computation | async-start | bytes 5505024 | tf_op jit(solution)/shard_map/all_to_all | solution.py:32
  39.5 62.7 %all-to-all-done = bf16[2,192,3584]{2,0,1:T(2,128)(2,1)} async-done(((bf16[2,192,3584]{2,0,1:T(2,128)(2,1)}), bf16[2,192,3584]{2,0,1:T(2,128)(2,1)}, u32[]{:S(2)}, u32[]{:S(2)}) %all-to-all-start) | async-done | bytes 2752544 | tf_op jit(solution)/shard_map/all_to_all | solution.py:32
  102.2 5.2 copy.30
  107.4 6.8 reshape.239
  114.2 2.8 fusion.27
  119.7 6.2 all-to-all-start.2
  126.7 4.2 copy.33
  131.0 4.3 all-to-all-done.2
  135.3 6.4 all-to-all-start.1
  141.8 124.8 %all_gather.24 = bf16[64,3584]{0,1:T(8,128)(2,1)S(1)} all-gather(bf16[64,56]{0,1:T(8,128)(2,1)S(1)} %fusion.38), channel_id=1, replica_groups=mesh['section'=8,'dp'=64] {'dp'}, dimensions={1}, use_global_device_ids=true | all-gather | bytes 465920 | tf_op jit(solution)/shard_map/all_gather | solution.py:96
  266.9 2.8 collective-permute-start
  270.4 2.3 collective-permute-done
  272.7 49.7 %all_gather.25 = bf16[64,3584]{0,1:T(8,128)(2,1)S(1)} all-gather(bf16[64,56]{0,1:T(8,128)(2,1)S(1)} %multiply_convert_fusion.6), channel_id=1, replica_groups=mesh['section'=8,'dp'=64] {'dp'}, dimensions={1}, use_global_device_ids=true | all-gather | bytes 465920 | tf_op jit(solution)/shard_map/all_gather | solution.py:96
  322.7 2.8 collective-permute-start.1
  326.2 2.9 collective-permute-done.1
  329.1 48.2 %all_gather.26 = bf16[64,3584]{0,1:T(8,128)(2,1)S(1)} all-gather(bf16[64,56]{0,1:T(8,128)(2,1)S(1)} %multiply_convert_fusion.5), channel_id=1, replica_groups=mesh['section'=8,'dp'=64] {'dp'}, dimensions={1}, use_global_device_ids=true | all-gather | bytes 465920 | tf_op jit(solution)/shard_map/all_gather | solution.py:96
  377.6 2.2 collective-permute-start.2
  380.5 4.1 collective-permute-done.2
  384.6 50.1 %all_gather.27 = bf16[64,3584]{0,1:T(8,128)(2,1)S(1)} all-gather(bf16[64,56]{0,1:T(8,128)(2,1)S(1)} %multiply_convert_fusion.4), channel_id=1, replica_groups=mesh['section'=8,'dp'=64] {'dp'}, dimensions={1}, use_global_device_ids=true | all-gather | bytes 465920 | tf_op jit(solution)/shard_map/all_gather | solution.py:96
  437.6 4.4 collective-permute-done.3
  442.0 48.2 %all_gather.28 = bf16[64,3584]{0,1:T(8,128)(2,1)S(1)} all-gather(bf16[64,56]{0,1:T(8,128)(2,1)S(1)} %multiply_convert_fusion.3), channel_id=1, replica_groups=mesh['section'=8,'dp'=64] {'dp'}, dimensions={1}, use_global_device_ids=true | all-gather | bytes 465920 | tf_op jit(solution)/shard_map/all_gather | solution.py:96
  493.1 4.4 collective-permute-done.4
  497.5 49.7 %all_gather.29 = bf16[64,3584]{0,1:T(8,128)(2,1)S(1)} all-gather(bf16[64,56]{0,1:T(8,128)(2,1)S(1)} %multiply_convert_fusion.2), channel_id=1, replica_groups=mesh['section'=8,'dp'=64] {'dp'}, dimensions={1}, use_global_device_ids=true | all-gather | bytes 465920 | tf_op jit(solution)/shard_map/all_gather | solution.py:96
  550.0 4.4 collective-permute-done.5
  554.5 48.3 %all_gather.30 = bf16[64,3584]{0,1:T(8,128)(2,1)S(1)} all-gather(bf16[64,56]{0,1:T(8,128)(2,1)S(1)} %multiply_convert_fusion.1), channel_id=1, replica_groups=mesh['section'=8,'dp'=64] {'dp'}, dimensions={1}, use_global_device_ids=true | all-gather | bytes 465920 | tf_op jit(solution)/shard_map/all_gather | solution.py:96
  605.7 4.4 collective-permute-done.6
  610.1 49.7 %all_gather.31 = bf16[64,3584]{0,1:T(8,128)(2,1)S(1)} all-gather(bf16[64,56]{0,1:T(8,128)(2,1)S(1)} %multiply_convert_fusion), channel_id=1, replica_groups=mesh['section'=8,'dp'=64] {'dp'}, dimensions={1}, use_global_device_ids=true | all-gather | bytes 465920 | tf_op jit(solution)/shard_map/all_gather | solution.py:96
  662.1 4.4 copy.34
  667.1 65.4 %all-reduce.1 = bf16[2,64,3584]{2,1,0:T(8,128)(2,1)} all-reduce(f32[2,64,3584]{2,1,0:T(8,128)S(1)} %convolution_bitcast_fusion), channel_id=1, replica_groups=mesh['section'=8,'dp'=64] {'section'}, use_global_device_ids=true, to_apply=%region_4.5 | all-reduce | flops 458752 | bytes 2752512 | tf_op jit(solution)/shard_map/psum | solution.py:82
  (63 shorter events, 23.9 us)
Async XLA Ops:
  0.6 113.6 %copy-start = (bf16[128,3584]{1,0:T(8,128)(2,1)S(1)}, bf16[128,3584]{1,0:T(8,128)(2,1)}, u32[]{:S(2)}) copy-start(bf16[128,3584]{1,0:T(8,128)(2,1)} %param.8) | copy-start | bytes 2752516
  23.5 14.2 %copy-start.5 = (f32[128,384]{1,0:T(8,128)S(1)}, f32[128,384]{1,0:T(8,128)}, u32[]{:S(2)}) copy-start(f32[128,384]{1,0:T(8,128)} %param.12) | copy-start | bytes 589828
  23.5 14.3 %copy-start.6 = (s32[64]{0:T(128)S(1)}, s32[64]{0:T(128)}, u32[]{:S(2)}) copy-start(s32[64]{0:T(128)} %param.11) | copy-start | bytes 772
  23.5 78.7 %all-to-all-start = ((bf16[2,192,3584]{2,0,1:T(2,128)(2,1)}), bf16[2,192,3584]{2,0,1:T(2,128)(2,1)}, u32[]{:S(2)}, u32[]{:S(2)}) async-start(bf16[2,192,3584]{2,0,1:T(2,128)(2,1)} %copy.29), calls=%async_computation | async-start | bytes 5505024 | tf_op jit(solution)/shard_map/all_to_all | solution.py:32
  114.2 3.1 copy-start.1
  119.7 15.6 %all-to-all-start.2 = ((f32[64,1,56]{2,1,0:T(1,128)}), f32[64,1,56]{2,1,0:T(1,128)S(1)}, u32[]{:S(2)}, u32[]{:S(2)}) async-start(f32[64,1,56]{2,1,0:T(1,128)} %bitcast.24), calls=%async_computation.2 | async-start | bytes 65536 | tf_op jit(solution)/shard_map/all_to_all | solution.py:71
  131.0 10.8 %copy-start.4 = (bf16[1,64,56]{1,2,0:T(8,128)(2,1)S(1)}, bf16[1,64,56]{1,2,0:T(8,128)(2,1)}, u32[]{:S(2)}) copy-start(bf16[1,64,56]{1,2,0:T(8,128)(2,1)} %param.15) | copy-start | bytes 21508
  131.0 135.7 %copy-start.2 = (bf16[1,56,3584]{2,1,0:T(8,128)(2,1)S(1)}, bf16[1,56,3584]{2,1,0:T(8,128)(2,1)}, u32[]{:S(2)}) copy-start(bf16[1,56,3584]{2,1,0:T(8,128)(2,1)} %param.13) | copy-start | bytes 1204228
  131.0 138.8 %copy-start.3 = (bf16[1,64,56]{1,2,0:T(8,128)(2,1)S(1)}, bf16[1,64,56]{1,2,0:T(8,128)(2,1)}, u32[]{:S(2)}) copy-start(bf16[1,64,56]{1,2,0:T(8,128)(2,1)} %param.14) | copy-start | bytes 21508
  135.3 526.8 %all-to-all-start.1 = ((bf16[128,3,3584]{2,1,0:T(4,128)(2,1)}), bf16[128,3,3584]{2,1,0:T(4,128)(2,1)}, u32[]{:S(2)}, u32[]{:S(2)}) async-start(bf16[128,3,3584]{2,1,0:T(4,128)(2,1)} %copy.33), calls=%async_computation.1 | async-start | bytes 7340032 | tf_op jit(solution)/shard_map/all_to_all | solution.py:70
  266.9 5.8 collective-permute-start
  322.7 6.4 collective-permute-start.1
  377.6 7.0 collective-permute-start.2
  435.0 7.0 collective-permute-start.3
  490.5 7.0 collective-permute-start.4
  547.4 7.0 collective-permute-start.5
  603.1 7.0 collective-permute-start.6
where the time goes:
time: 742 us; the launch traced here: 733 us
  blocking collectives  534 us (72%)
  waiting for transfers between devices  93.9 us (13%)
  local copies, waits for them, and re-layouts  42.9 us (6%)
  starting transfers between devices  42.2 us (6%)
  matrix products  14.8 us (2%)
    all_gather x8, blocking collectives, body(): piece = lax.all_gather(inner, 'dp', axis=1, tiled=True)  469 us
    psum x1, blocking collectives, body(): passage_out = lax.psum(dense, 'section').astype(jnp.bfloat16)  65.4 us
    all_to_all x1, waiting for transfers between devices, body(): lax.all_to_all(outgoing, 'dp', split_axis=1, concat_axis=0, tiled=True)  62.7 us
    ppermute x7, waiting for transfers between devices, passed_along(): lax.ppermute(value, axis, [(source, source + steps) for source in range(i...  26.8 us
    ppermute x7, starting transfers between devices, passed_along(): lax.ppermute(value, axis, [(source, source + steps) for source in range(i...  15.5 us
    gather x1, local copies, waits for them, and re-layouts, body(): outgoing = jnp.take(passages, all_slots, axis=1)  15.2 us
  transfers between devices with their start and end apart: 10, of which 9 were waited for; matrix products, arithmetic and copies ran while one was open for 2% of the time, Pallas kernels for 0%

commit v1 on v0

--- a/solution.py
+++ b/solution.py
@@ -79,7 +79,7 @@
         precision=lax.Precision.HIGHEST,
         preferred_element_type=jnp.float32,
     )
-    passage_out = lax.psum(dense, "section").astype(jnp.bfloat16)
+    passage_out = jnp.sum(lax.all_gather(dense, "section"), axis=0).astype(jnp.bfloat16)
     weight_rows = section_weights[0]
     input_cols = section_inputs[0]
     pre = pre_acts[0].astype(jnp.float32)

time: 742 us -> 713 us (0.961)
  the two profiles are of different devices: /device:TPU:16 before, /device:TPU:25 now
where the time goes in v1:
time: 713 us; the launch traced here: 704 us
  blocking collectives  490 us (69%)
  waiting for transfers between devices  97.1 us (14%)
  local copies, waits for them, and re-layouts  39.1 us (5%)
  starting transfers between devices  33.9 us (5%)
  matrix products  17.7 us (2%)
  between operations  14.6 us (2%)
  other arithmetic  11.2 us (2%)
    all_gather x8, blocking collectives, body(): piece = lax.all_gather(inner, 'dp', axis=1, tiled=True)  400 us
    all_to_all x1, blocking collectives, body(): lax.all_to_all(block_terms, 'dp', split_axis=0, concat_axis=1, tiled=True)  90.5 us
    all_to_all x1, waiting for transfers between devices, body(): lax.all_to_all(outgoing, 'dp', split_axis=1, concat_axis=0, tiled=True)  63.2 us
    ppermute x7, waiting for transfers between devices, passed_along(): lax.ppermute(value, axis, [(source, source + steps) for source in range(i...  24.7 us
    gather x1, local copies, waits for them, and re-layouts, body(): outgoing = jnp.take(passages, all_slots, axis=1)  15.2 us
    all_to_all x1, starting transfers between devices, body(): lax.all_to_all(outgoing, 'dp', split_axis=1, concat_axis=0, tiled=True)  14.3 us
  transfers between devices with their start and end apart: 10, of which 9 were waited for; matrix products, arithmetic and copies ran while one was open for 2% of the time, Pallas kernels for 0%

profile of v1, /device:TPU:25, one launch (start us, length us, event | category | flops | bytes accessed | tf_op | source)
XLA Modules:
  0.0 704.0 jit_solution(14964517737946096358)
XLA Ops:
  8.3 15.2 %gather_fusion = bf16[192,2,3584]{2,0,1:T(8,128)(2,1)} fusion(bf16[2,64,3584]{2,1,0:T(8,128)(2,1)} %param.9, s32[1024]{0:T(1024)S(1)} %pad_clamp_fusion), kind=kCustom, calls=%fused_computation | custom fusion | bytes 5505792 | tf_op jit(solution)/shard_map/jit(_take)/gather | solution.py:31
  23.6 2.1 select_bitcast_fusion
  25.7 4.4 copy.29
  30.1 14.3 %all-to-all-start = ((bf16[2,192,3584]{2,0,1:T(2,128)(2,1)}), bf16[2,192,3584]{2,0,1:T(2,128)(2,1)}, u32[]{:S(2)}, u32[]{:S(2)}) async-start(bf16[2,192,3584]{2,0,1:T(2,128)(2,1)} %copy.29), calls=%async_computation | async-start | bytes 5505024 | tf_op jit(solution)/shard_map/all_to_all | solution.py:32
  46.2 63.2 %all-to-all-done = bf16[2,192,3584]{2,0,1:T(2,128)(2,1)} async-done(((bf16[2,192,3584]{2,0,1:T(2,128)(2,1)}), bf16[2,192,3584]{2,0,1:T(2,128)(2,1)}, u32[]{:S(2)}, u32[]{:S(2)}) %all-to-all-start) | async-done | bytes 2752544 | tf_op jit(solution)/shard_map/all_to_all | solution.py:32
  109.4 5.2 copy.30
  114.7 6.8 reshape.239
  121.4 2.7 fusion.27
  125.3 2.4 copy.33
  127.7 90.5 %all_to_all.42 = bf16[128,3,3584]{2,1,0:T(4,128)(2,1)S(1)} all-to-all(bf16[128,3,3584]{2,1,0:T(4,128)(2,1)S(1)} %copy.33), channel_id=1, replica_groups=mesh['section'=8,'dp'=64] {'dp'}, dimensions={0} | all-to-all | bytes 5505024 | tf_op jit(solution)/shard_map/all_to_all | solution.py:70
  218.1 2.4 copy.34
  222.4 3.4 fusion.47
  226.6 6.1 all-to-all-start.2
  232.7 9.2 %all-to-all-done.2 = f32[64,1,56]{2,1,0:T(1,128)S(1)} async-done(((f32[64,1,56]{2,1,0:T(1,128)}), f32[64,1,56]{2,1,0:T(1,128)S(1)}, u32[]{:S(2)}, u32[]{:S(2)}) %all-to-all-start.2) | async-done | bytes 14368 | tf_op jit(solution)/shard_map/all_to_all | solution.py:71
  242.1 48.9 %all_gather.32 = bf16[64,3584]{0,1:T(8,128)(2,1)S(1)} all-gather(bf16[64,56]{0,1:T(8,128)(2,1)S(1)} %fusion.38), channel_id=1, replica_groups=mesh['section'=8,'dp'=64] {'dp'}, dimensions={1}, use_global_device_ids=true | all-gather | bytes 465920 | tf_op jit(solution)/shard_map/all_gather | solution.py:96
  291.2 1.9 collective-permute-start
  293.8 4.3 collective-permute-done
  298.2 50.2 %all_gather.33 = bf16[64,3584]{0,1:T(8,128)(2,1)S(1)} all-gather(bf16[64,56]{0,1:T(8,128)(2,1)S(1)} %multiply_convert_fusion.6), channel_id=1, replica_groups=mesh['section'=8,'dp'=64] {'dp'}, dimensions={1}, use_global_device_ids=true | all-gather | bytes 465920 | tf_op jit(solution)/shard_map/all_gather | solution.py:96
  348.7 1.9 collective-permute-start.1
  351.3 4.3 collective-permute-done.1
  355.6 49.5 %all_gather.34 = bf16[64,3584]{0,1:T(8,128)(2,1)S(1)} all-gather(bf16[64,56]{0,1:T(8,128)(2,1)S(1)} %multiply_convert_fusion.5), channel_id=1, replica_groups=mesh['section'=8,'dp'=64] {'dp'}, dimensions={1}, use_global_device_ids=true | all-gather | bytes 465920 | tf_op jit(solution)/shard_map/all_gather | solution.py:96
  408.0 3.2 collective-permute-done.2
  411.3 50.7 %all_gather.35 = bf16[64,3584]{0,1:T(8,128)(2,1)S(1)} all-gather(bf16[64,56]{0,1:T(8,128)(2,1)S(1)} %multiply_convert_fusion.4), channel_id=1, replica_groups=mesh['section'=8,'dp'=64] {'dp'}, dimensions={1}, use_global_device_ids=true | all-gather | bytes 465920 | tf_op jit(solution)/shard_map/all_gather | solution.py:96
  464.8 3.2 collective-permute-done.3
  468.1 49.5 %all_gather.36 = bf16[64,3584]{0,1:T(8,128)(2,1)S(1)} all-gather(bf16[64,56]{0,1:T(8,128)(2,1)S(1)} %multiply_convert_fusion.3), channel_id=1, replica_groups=mesh['section'=8,'dp'=64] {'dp'}, dimensions={1}, use_global_device_ids=true | all-gather | bytes 465920 | tf_op jit(solution)/shard_map/all_gather | solution.py:96
  520.5 3.2 collective-permute-done.4
  523.7 50.8 %all_gather.37 = bf16[64,3584]{0,1:T(8,128)(2,1)S(1)} all-gather(bf16[64,56]{0,1:T(8,128)(2,1)S(1)} %multiply_convert_fusion.2), channel_id=1, replica_groups=mesh['section'=8,'dp'=64] {'dp'}, dimensions={1}, use_global_device_ids=true | all-gather | bytes 465920 | tf_op jit(solution)/shard_map/all_gather | solution.py:96
  577.4 3.2 collective-permute-done.5
  580.7 49.5 %all_gather.38 = bf16[64,3584]{0,1:T(8,128)(2,1)S(1)} all-gather(bf16[64,56]{0,1:T(8,128)(2,1)S(1)} %multiply_convert_fusion.1), channel_id=1, replica_groups=mesh['section'=8,'dp'=64] {'dp'}, dimensions={1}, use_global_device_ids=true | all-gather | bytes 465920 | tf_op jit(solution)/shard_map/all_gather | solution.py:96
  633.1 3.2 collective-permute-done.6
  636.3 50.7 %all_gather.39 = bf16[64,3584]{0,1:T(8,128)(2,1)S(1)} all-gather(bf16[64,56]{0,1:T(8,128)(2,1)S(1)} %multiply_convert_fusion), channel_id=1, replica_groups=mesh['section'=8,'dp'=64] {'dp'}, dimensions={1}, use_global_device_ids=true | all-gather | bytes 465920 | tf_op jit(solution)/shard_map/all_gather | solution.py:96
  689.3 7.7 %reduce_sum.29 = bf16[2,64,3584]{2,1,0:T(8,128)(2,1)} reduce(f32[8,2,64,3584]{3,2,1,0:T(8,128)} %bitcast.160, f32[]{:T(128)} %constant.9.clone.1), dimensions={0}, to_apply=%region_4.5 | reduce | flops 3211264 | bytes 15597572 | tf_op jit(solution)/shard_map/reduce_sum | solution.py:82
  (63 shorter events, 25.5 us)
Async XLA Ops:
  7.2 114.3 %copy-start = (bf16[128,3584]{1,0:T(8,128)(2,1)S(1)}, bf16[128,3584]{1,0:T(8,128)(2,1)}, u32[]{:S(2)}) copy-start(bf16[128,3584]{1,0:T(8,128)(2,1)} %param.8) | copy-start | bytes 2752516
  30.1 14.4 %copy-start.4 = (f32[128,384]{1,0:T(8,128)S(1)}, f32[128,384]{1,0:T(8,128)}, u32[]{:S(2)}) copy-start(f32[128,384]{1,0:T(8,128)} %param.12) | copy-start | bytes 589828
  30.1 14.5 %copy-start.5 = (s32[64]{0:T(128)S(1)}, s32[64]{0:T(128)}, u32[]{:S(2)}) copy-start(s32[64]{0:T(128)} %param.11) | copy-start | bytes 772
  30.1 79.3 %all-to-all-start = ((bf16[2,192,3584]{2,0,1:T(2,128)(2,1)}), bf16[2,192,3584]{2,0,1:T(2,128)(2,1)}, u32[]{:S(2)}, u32[]{:S(2)}) async-start(bf16[2,192,3584]{2,0,1:T(2,128)(2,1)} %copy.29), calls=%async_computation | async-start | bytes 5505024 | tf_op jit(solution)/shard_map/all_to_all | solution.py:32
  44.4 644.9 %all-gather.3.cloned.1.call-start = ((), (), s32[]{:S(2)}) async-start(), calls=%async_computation.3 | async-start | bytes 16515072 | tf_op jit(solution)/shard_map/all_gather | solution.py:82
  222.4 19.6 %copy-start.3 = (bf16[1,64,56]{1,2,0:T(8,128)(2,1)S(1)}, bf16[1,64,56]{1,2,0:T(8,128)(2,1)}, u32[]{:S(2)}) copy-start(bf16[1,64,56]{1,2,0:T(8,128)(2,1)} %param.15) | copy-start | bytes 21508
  222.4 68.5 %copy-start.1 = (bf16[1,56,3584]{2,1,0:T(8,128)(2,1)S(1)}, bf16[1,56,3584]{2,1,0:T(8,128)(2,1)}, u32[]{:S(2)}) copy-start(bf16[1,56,3584]{2,1,0:T(8,128)(2,1)} %param.13) | copy-start | bytes 1204228
  222.4 70.8 %copy-start.2 = (bf16[1,64,56]{1,2,0:T(8,128)(2,1)S(1)}, bf16[1,64,56]{1,2,0:T(8,128)(2,1)}, u32[]{:S(2)}) copy-start(bf16[1,64,56]{1,2,0:T(8,128)(2,1)} %param.14) | copy-start | bytes 21508
  226.6 15.4 %all-to-all-start.2 = ((f32[64,1,56]{2,1,0:T(1,128)}), f32[64,1,56]{2,1,0:T(1,128)S(1)}, u32[]{:S(2)}, u32[]{:S(2)}) async-start(f32[64,1,56]{2,1,0:T(1,128)} %bitcast.25), calls=%async_computation.2 | async-start | bytes 65536 | tf_op jit(solution)/shard_map/all_to_all | solution.py:71
  291.2 6.9 collective-permute-start
  348.7 6.9 collective-permute-start.1
  405.4 5.8 collective-permute-start.2
  462.2 5.8 collective-permute-start.3
  517.9 5.8 collective-permute-start.4
  574.8 5.8 collective-permute-start.5
  630.5 5.8 collective-permute-start.6
Sparse Core Ops, SparseCore 0:
  222.5 152.9 all-gather.2
